TPU v7x, 512 devices: a whole 4x4x16 slice. The times are simulated.
512 devices in a mesh: section: 32 (over z_lo, y, core), seq: 16 (over x, z_hi).
Axes of the slice: x: 4, y: 4, z: 16 (z_hi: 4, z_lo: 4; z = z_hi * 4 + z_lo), core: 2. Of those that a mesh axis runs over, the one named last changes fastest.
Arguments:
- up_activation: bfloat16 [32, 2048, 4096], P('section', 'seq'), as said below
- saved_projections: bfloat16 [32, 2048, 768], P('section', 'seq'), as said below
- up_cotangent: bfloat16 [32, 2048, 4096], P('section', 'seq'), may hold values from -6 to 6
- up_input_weight: bfloat16 [32, 4096, 768], P('section', 'seq'), may hold values from -0.09375 to 0.09375
- up_output_weight: bfloat16 [32, 512, 4096], P('section', None, 'seq'), may hold values from -0.25 to 0.25
- upward_gain: float32 [32, 4096], P('section'), may hold values from 0.5 to 1.5
- accum_input: bfloat16 [32, 4096, 768], P('section', 'seq'), may hold values from -48 to 48
- doc_starts: int32 [32, 2048], P('section', 'seq'), may hold values from 0 to 2047, as said below
Outputs:
- upward_grad: bfloat16 [32, 2048, 4096], P('section', 'seq')
- project_grads: bfloat16 [32, 4096, 768], P('section', 'seq')
Inputs may be any that keep to these rules, and one draw needn't show every extreme that they name: doc_starts[s, t] is the position of the first token of the document holding token t: it is 0 at t = 0, equals t or doc_starts[s, t - 1] elsewhere, and the last token of every micro-batch starts a document. `up_activation`: saved inputs of the upward layers. `saved_projections`: saved queries, keys and values of the upward layers.
All inputs are finite; a program needn't handle non-finite values.
Results may differ from a plain program's by a relative error of at most 0.014.
Values may be sent and summed in bfloat16 or wider, within the bound.
No kernel may reach another device: no remote copies, remote signals or barrier semaphores. Data moves between devices by JAX's collectives and lax.ppermute only.
A program may use at most 64 MiB of HBM per device.

v0:
```python
import jax
import jax.numpy as jnp
from jax import lax
from jax.sharding import PartitionSpec as P

HEAD = 128
GROUP = 4
INNER = 4


def shifted(value, axis, steps):
    count = lax.axis_size(axis)
    initial, last = (max(0, -steps), min(count, count - steps))
    return lax.ppermute(value, axis, [(source, source + steps) for source in range(initial, last)])


def mirrored(value, axis):
    count = lax.axis_size(axis)
    return lax.ppermute(value, axis, [(source, count - 1 - source) for source in range(count)])


def seq_pairs(shift, level):
    size = lax.axis_size("seq")
    outer = size // INNER
    if level == 0:
        return [
            (o * INNER + i, o * INNER + (i + shift) % INNER)
            for o in range(outer)
            for i in range(INNER)
        ]
    return [
        (o * INNER + i, (o + shift) % outer * INNER + i) for o in range(outer) for i in range(INNER)
    ]


def gather_blocks(x):
    outer = lax.axis_size("seq") // INNER
    first = jnp.stack([x] + [lax.ppermute(x, "seq", seq_pairs(k, 0)) for k in range(1, INNER)])
    return jnp.stack(
        [first] + [lax.ppermute(first, "seq", seq_pairs(k, 1)) for k in range(1, outer)]
    )


def reduce_blocks(y, wire):
    outer = lax.axis_size("seq") // INNER
    acc = y[0]
    for k in range(1, outer):
        acc = acc + lax.ppermute(y[k].astype(wire), "seq", seq_pairs(outer - k, 1)).astype(y.dtype)
    total = acc[0]
    for k in range(1, INNER):
        total = total + lax.ppermute(acc[k].astype(wire), "seq", seq_pairs(INNER - k, 0)).astype(
            y.dtype
        )
    return total


def gather_and_scatter(x, cols, o, i):
    outer = lax.axis_size("seq") // INNER
    m, n, w = x.shape
    parts = cols.reshape(n, outer, INNER, w).transpose(2, 1, 0, 3)
    first = [jnp.concatenate([x, parts[i]])]
    for k in range(1, INNER):
        piece = lax.dynamic_index_in_dim(parts, (i + k) % INNER, 0, keepdims=False)
        first.append(lax.ppermute(jnp.concatenate([x, piece]), "seq", seq_pairs(k, 0)))
    first = jnp.stack(first, axis=1)
    own, rest = (first[:m], first[m:])
    second = []
    for k in range(1, outer):
        piece = lax.dynamic_index_in_dim(rest, (o + k) % outer, 0, keepdims=False)
        payload = jnp.concatenate([own.reshape(m * INNER, n, w), piece])
        second.append(lax.ppermute(payload, "seq", seq_pairs(k, 1)))
    gathered = jnp.stack([own] + [s[: m * INNER].reshape(m, INNER, n, w) for s in second])
    scattered = jnp.stack(
        [lax.dynamic_index_in_dim(rest, o, 0, keepdims=False)] + [s[m * INNER :] for s in second]
    )
    return (gathered, scattered)


def gather_columns(y, o, i):
    outer = lax.axis_size("seq") // INNER
    n, w = (y.shape[2], y.shape[3])
    first = [y[0]]
    for k in range(1, outer):
        first.append(lax.ppermute(y[k], "seq", seq_pairs(outer - k, 1)))
    first = jnp.stack(first, axis=1)
    second = [first[0]]
    for k in range(1, INNER):
        second.append(lax.ppermute(first[k], "seq", seq_pairs(INNER - k, 0)))
    second = jnp.stack(second, axis=1)
    second = jnp.roll(jnp.roll(second, o, axis=0), i, axis=1)
    return second.transpose(2, 0, 1, 3).reshape(n, outer * INNER * w)


def contract_last(left, right):
    return lax.dot_general(
        left, right, (((1,), (1,)), ((), ())), preferred_element_type=jnp.float32
    )


def contract_first(left, right):
    return lax.dot_general(
        left, right, (((0,), (0,)), ((), ())), preferred_element_type=jnp.float32
    )


def normalize(values, gain):
    floats = values.astype(jnp.float32)
    inverse = lax.rsqrt(jnp.mean(floats * floats, axis=-1, keepdims=True) + 1e-05)
    unit = floats * inverse
    return (unit, inverse, unit * gain)


def per_device(
    up_activation,
    saved_projections,
    up_cotangent,
    up_input_weight,
    up_output_weight,
    upward_gain,
    accum_input,
    doc_starts,
):
    factor = HEAD ** (-0.5)
    width = GROUP * HEAD
    count = up_activation.shape[1]
    size = lax.axis_size("seq")
    outer = size // INNER
    me = lax.axis_index("seq")
    o, i = (me // INNER, me % INNER)
    first = me * count
    saved = saved_projections[0]
    cotangent = up_cotangent[0]
    unit_up, inverse_up, normed_up = normalize(up_activation[0], upward_gain[0])
    hidden = normed_up.astype(jnp.bfloat16)
    output_weight = lax.all_gather(up_output_weight[0], "seq", axis=1, tiled=True)
    key_value = gather_blocks(saved[:, width:]).reshape(size * count, 2 * HEAD)
    kv_weight_all = lax.all_gather(up_input_weight[0][:, width:], "seq", axis=0, tiled=True)
    keys = key_value[:, :HEAD]
    values = key_value[:, HEAD:]
    sources = (
        ((o - jnp.arange(outer, dtype=jnp.int32)) % outer)[:, None] * INNER
        + ((i - jnp.arange(INNER, dtype=jnp.int32)) % INNER)[None, :]
    ).reshape(size)
    key_positions = (
        sources[:, None] * count + jnp.arange(count, dtype=jnp.int32)[None, :]
    ).reshape(-1)
    query = saved[:, :width].reshape(count, GROUP, HEAD)
    attn_grad = contract_last(cotangent, output_weight).astype(jnp.bfloat16)
    positions = first + jnp.arange(count, dtype=jnp.int32)
    starts = doc_starts[0]
    visible = (key_positions[None, :] <= positions[:, None]) & (
        key_positions[None, :] >= starts[:, None]
    )
    scores = jnp.einsum("tgh,jh->tgj", query, keys, preferred_element_type=jnp.float32) * factor
    scores = jnp.where(visible[:, None, :], scores, -1e30)
    top = jnp.max(scores, axis=-1, keepdims=True)
    exps = jnp.where(visible[:, None, :], jnp.exp(scores - top), 0.0)
    probs = exps / jnp.sum(exps, axis=-1, keepdims=True)
    weights = probs.astype(jnp.bfloat16)
    grad_heads = attn_grad.reshape(count, GROUP, HEAD)
    prob_grad = jnp.einsum("tgh,jh->tgj", grad_heads, values, preferred_element_type=jnp.float32)
    inner = jnp.sum(probs * prob_grad, axis=-1, keepdims=True)
    score_grad = (probs * (prob_grad - inner) * factor).astype(jnp.bfloat16)
    query_grad = (
        jnp.einsum("tgj,jh->tgh", score_grad, keys, preferred_element_type=jnp.float32)
        .astype(jnp.bfloat16)
        .reshape(count, width)
    )
    key_part = jnp.einsum("tgj,tgh->jh", score_grad, query, preferred_element_type=jnp.float32)
    value_part = jnp.einsum("tgj,tgh->jh", weights, grad_heads, preferred_element_type=jnp.float32)
    kv_part = jnp.concatenate([key_part, value_part], axis=1).reshape(outer, INNER, count, 2 * HEAD)
    query_all = gather_blocks(query_grad)
    kv_grad = reduce_blocks(kv_part, jnp.bfloat16).astype(jnp.bfloat16)
    kv_all, hidden_cols = gather_and_scatter(kv_grad[None], hidden, o, i)
    hidden_cols = hidden_cols.reshape(size * count, -1)
    grad_all = jnp.concatenate([query_all, kv_all[:, 0]], axis=-1).reshape(size * count, -1)
    input_term = contract_first(hidden_cols, grad_all).astype(jnp.bfloat16)
    block = contract_last(query_all.reshape(size * count, -1), up_input_weight[0][:, :width])
    hidden_grad = gather_columns(block.astype(jnp.bfloat16).reshape(outer, INNER, count, -1), o, i)
    hidden_grad = hidden_grad.astype(jnp.float32) + contract_last(kv_grad, kv_weight_all)
    scaled = hidden_grad * upward_gain[0]
    input_grad = cotangent.astype(jnp.float32) + inverse_up * (
        scaled - unit_up * jnp.mean(scaled * unit_up, axis=-1, keepdims=True)
    )
    moved_grad = shifted(input_grad.astype(jnp.bfloat16), "section", 1)
    mirror_input = mirrored(input_term, "section")
    project_grads = (accum_input[0].astype(jnp.float32) + mirror_input.astype(jnp.float32)).astype(
        jnp.bfloat16
    )
    return (moved_grad[None], project_grads[None])


def solution(mesh):
    return jax.shard_map(
        per_device,
        mesh=mesh,
        in_specs=(
            P("section", "seq", None),
            P("section", "seq", None),
            P("section", "seq", None),
            P("section", "seq", None),
            P("section", None, "seq"),
            P("section", None),
            P("section", "seq", None),
            P("section", "seq"),
        ),
        out_specs=(P("section", "seq", None), P("section", "seq", None)),
        check_vma=False,
    )
```

profile of v0, /device:TPU:43, one launch (start us, length us, event | category | flops | bytes accessed | tf_op | source)
XLA Modules:
  0.0 437.8 jit_solution(3843633651568549297)
XLA Ops:
  9.1 8.8 %collective-permute-start = (bf16[128,256]{0,1:T(8,128)(2,1)S(1)}, bf16[128,256]{0,1:T(8,128)(2,1)S(1)}, u32[]{:S(2)}, u32[]{:S(2)}) collective-permute-start(bf16[128,256]{0,1:T(8,128)(2,1)S(1)} %get-tuple-element.40), channel_id=1, source_target_pairs={{0,1},{1,2},{2,3},{3,0},{4,5},{5,6},{6,7},{7,4},{8,9},{9,10},{10,1... | collective-permute-start | bytes 196616 | tf_op jit(solution)/shard_map/ppermute | solution.py:38
  17.9 9.7 %collective-permute-start.1 = (bf16[128,256]{0,1:T(8,128)(2,1)S(1)}, bf16[128,256]{0,1:T(8,128)(2,1)S(1)}, u32[]{:S(2)}, u32[]{:S(2)}) collective-permute-start(bf16[128,256]{0,1:T(8,128)(2,1)S(1)} %get-tuple-element.40), channel_id=1, source_target_pairs={{0,2},{1,3},{2,0},{3,1},{4,6},{5,7},{6,4},{7,5},{8,10},{9,11},{10,... | collective-permute-start | bytes 196616 | tf_op jit(solution)/shard_map/ppermute | solution.py:38
  34.7 5.3 %collective-permute-done.2 = bf16[128,256]{0,1:T(8,128)(2,1)S(1)} collective-permute-done((bf16[128,256]{0,1:T(8,128)(2,1)S(1)}, bf16[128,256]{0,1:T(8,128)(2,1)S(1)}, u32[]{:S(2)}, u32[]{:S(2)}) %collective-permute-start.2) | collective-permute-done | bytes 65568 | tf_op jit(solution)/shard_map/ppermute | solution.py:38
  53.6 6.2 %collective-permute-done.5 = bf16[4,128,256]{1,2,0:T(8,128)(2,1)S(1)} collective-permute-done((bf16[4,128,256]{1,2,0:T(8,128)(2,1)S(1)}, bf16[4,128,256]{1,2,0:T(8,128)(2,1)S(1)}, u32[]{:S(2)}, u32[]{:S(2)}) %collective-permute-start.5) | collective-permute-done | bytes 262176 | tf_op jit(solution)/shard_map/ppermute | solution.py:40
  64.2 80.2 %all-gather.6.cloned.1.call-done = bf16[1,512,4096]{2,1,0:T(8,128)(2,1)} async-done(((bf16[1,512,256]{2,1,0:T(8,128)(2,1)}), bf16[1,512,4096]{2,1,0:T(8,128)(2,1)}) %all-gather.6.cloned.1.call-update) | async-done | bytes 4194320 | tf_op jit(solution)/shard_map/all_gather | solution.py:135
  152.7 7.6 %convolution_bitcast_fusion.1 = f32[2048,128]{0,1:T(8,128)S(1)} fusion(bf16[128,4,128]{0,2,1:T(8,128)(2,1)S(1)} %bitcast.230, f32[128,4,2048]{0,2,1:T(8,128)} %fusion.64, f32[128,4,2048]{0,2,1:T(8,128)} %get-tuple-element.46, f32[128,4]{0,1:T(4,128)S(1)} %get-tuple-element.45), kind=kOutput, calls=%fused_computation.27 | convolution fusion | flops 275778048 | bytes 9570304 | tf_op jit(solution)/shard_map/tgj,tgh->jh/dot_general | solution.py:169
  160.3 7.6 %fusion.41 = bf16[128,4,128]{0,2,1:T(8,128)(2,1)S(1)} fusion(f32[128,4,2048]{0,2,1:T(8,128)} %fusion.64, bf16[2048,256]{1,0:T(8,128)(2,1)} %bitcast.196, f32[128,4,2048]{0,2,1:T(8,128)} %get-tuple-element.46, f32[128,4]{0,1:T(4,128)S(1)} %get-tuple-element.45), kind=kOutput, calls=%fused_computation.59 | convolution fusion | flops 275843584 | bytes 17436672 | tf_op jit(solution)/shard_map/tgj,jh->tgh/dot_general | solution.py:165
  172.2 6.4 %collective-permute-start.7 = (bf16[128,512]{1,0:T(8,128)(2,1)}, bf16[128,512]{1,0:T(8,128)(2,1)}, u32[]{:S(2)}, u32[]{:S(2)}) collective-permute-start(bf16[128,512]{1,0:T(8,128)(2,1)} %copy.48), channel_id=1, source_target_pairs={{0,2},{1,3},{2,0},{3,1},{4,6},{5,7},{6,4},{7,5},{8,10},{9,11},{10,... | collective-permute-start | bytes 393224 | tf_op jit(solution)/shard_map/ppermute | solution.py:38
  178.6 6.7 %collective-permute-start.8 = (bf16[128,512]{1,0:T(8,128)(2,1)}, bf16[128,512]{1,0:T(8,128)(2,1)}, u32[]{:S(2)}, u32[]{:S(2)}) collective-permute-start(bf16[128,512]{1,0:T(8,128)(2,1)} %copy.48), channel_id=1, source_target_pairs={{0,3},{1,0},{2,1},{3,2},{4,7},{5,4},{6,5},{7,6},{8,11},{9,8},{10,9... | collective-permute-start | bytes 393224 | tf_op jit(solution)/shard_map/ppermute | solution.py:38
  224.5 6.4 %collective-permute-start.22 = (bf16[128,256]{1,0:T(8,128)(2,1)S(1)}, bf16[128,256]{1,0:T(8,128)(2,1)S(1)}, u32[]{:S(2)}, u32[]{:S(2)}) collective-permute-start(bf16[128,256]{1,0:T(8,128)(2,1)S(1)} %get-tuple-element.36), channel_id=1, source_target_pairs={{0,2},{1,3},{2,0},{3,1},{4,6},{5,7},{6,4},{7,5},{8,10},{9,11},{10,... | collective-permute-start | bytes 196616 | tf_op jit(solution)/shard_map/ppermute | solution.py:51
  230.9 6.5 %collective-permute-start.23 = (bf16[128,256]{1,0:T(8,128)(2,1)S(1)}, bf16[128,256]{1,0:T(8,128)(2,1)S(1)}, u32[]{:S(2)}, u32[]{:S(2)}) collective-permute-start(bf16[128,256]{1,0:T(8,128)(2,1)S(1)} %get-tuple-element.35), channel_id=1, source_target_pairs={{0,1},{1,2},{2,3},{3,0},{4,5},{5,6},{6,7},{7,4},{8,9},{9,10},{10,1... | collective-permute-start | bytes 196616 | tf_op jit(solution)/shard_map/ppermute | solution.py:51
  238.9 5.3 %collective-permute-done.22 = bf16[128,256]{1,0:T(8,128)(2,1)S(1)} collective-permute-done((bf16[128,256]{1,0:T(8,128)(2,1)S(1)}, bf16[128,256]{1,0:T(8,128)(2,1)S(1)}, u32[]{:S(2)}, u32[]{:S(2)}) %collective-permute-start.22) | collective-permute-done | bytes 65568 | tf_op jit(solution)/shard_map/ppermute | solution.py:51
  245.2 12.0 %collective-permute-start.25 = (bf16[5,128,256]{2,1,0:T(8,128)(2,1)S(1)}, bf16[5,128,256]{2,1,0:T(8,128)(2,1)S(1)}, u32[]{:S(2)}, u32[]{:S(2)}) collective-permute-start(bf16[5,128,256]{2,1,0:T(8,128)(2,1)S(1)} %get-tuple-element.42), channel_id=1, source_target_pairs={{0,1},{1,2},{2,3},{3,0},{4,5},{5,6},{6,7},{7,4},{8,9},{9,10},{10,1... | collective-permute-start | bytes 983048 | tf_op jit(solution)/shard_map/ppermute | solution.py:64
  257.2 8.0 %collective-permute-start.26 = (bf16[5,128,256]{2,1,0:T(8,128)(2,1)S(1)}, bf16[5,128,256]{2,1,0:T(8,128)(2,1)S(1)}, u32[]{:S(2)}, u32[]{:S(2)}) collective-permute-start(bf16[5,128,256]{2,1,0:T(8,128)(2,1)S(1)} %get-tuple-element.43), channel_id=1, source_target_pairs={{0,2},{1,3},{2,0},{3,1},{4,6},{5,7},{6,4},{7,5},{8,10},{9,11},{10,... | collective-permute-start | bytes 983048 | tf_op jit(solution)/shard_map/ppermute | solution.py:64
  271.6 5.7 %collective-permute-start.13 = (bf16[4,128,256]{2,1,0:T(8,128)(2,1)S(1)}, bf16[4,128,256]{2,1,0:T(8,128)(2,1)S(1)}, u32[]{:S(2)}, u32[]{:S(2)}) collective-permute-start(bf16[4,128,256]{2,1,0:T(8,128)(2,1)S(1)} %bitcast.221), channel_id=1, source_target_pairs={{0,8},{1,9},{2,10},{3,11},{4,12},{5,13},{6,14},{7,15},{8,0},{9,1},... | collective-permute-start | bytes 786440 | tf_op jit(solution)/shard_map/ppermute | solution.py:84
  277.3 17.4 %collective-permute-done.25 = bf16[5,128,256]{2,1,0:T(8,128)(2,1)S(1)} collective-permute-done((bf16[5,128,256]{2,1,0:T(8,128)(2,1)S(1)}, bf16[5,128,256]{2,1,0:T(8,128)(2,1)S(1)}, u32[]{:S(2)}, u32[]{:S(2)}) %collective-permute-start.25) | collective-permute-done | bytes 327712 | tf_op jit(solution)/shard_map/ppermute | solution.py:64
  294.7 5.9 %collective-permute-start.14 = (bf16[4,128,256]{2,1,0:T(8,128)(2,1)S(1)}, bf16[4,128,256]{2,1,0:T(8,128)(2,1)S(1)}, u32[]{:S(2)}, u32[]{:S(2)}) collective-permute-start(bf16[4,128,256]{2,1,0:T(8,128)(2,1)S(1)} %bitcast.219), channel_id=1, source_target_pairs={{0,4},{1,5},{2,6},{3,7},{4,8},{5,9},{6,10},{7,11},{8,12},{9,13},{1... | collective-permute-start | bytes 786440 | tf_op jit(solution)/shard_map/ppermute | solution.py:84
  316.1 5.4 %collective-permute-start.17 = (bf16[4,128,256]{2,1,0:T(8,128)(2,1)S(1)}, bf16[4,128,256]{2,1,0:T(8,128)(2,1)S(1)}, u32[]{:S(2)}, u32[]{:S(2)}) collective-permute-start(bf16[4,128,256]{2,1,0:T(8,128)(2,1)S(1)} %get-tuple-element.15), channel_id=1, source_target_pairs={{0,1},{1,2},{2,3},{3,0},{4,5},{5,6},{6,7},{7,4},{8,9},{9,10},{10,1... | collective-permute-start | bytes 786440 | tf_op jit(solution)/shard_map/ppermute | solution.py:88
  323.5 6.1 %collective-permute-start.28 = (bf16[8,128,256]{2,1,0:T(8,128)(2,1)}, bf16[8,128,256]{2,1,0:T(8,128)(2,1)}, u32[]{:S(2)}, u32[]{:S(2)}) collective-permute-start(bf16[8,128,256]{2,1,0:T(8,128)(2,1)} %get-tuple-element.31), channel_id=1, source_target_pairs={{0,4},{1,5},{2,6},{3,7},{4,8},{5,9},{6,10},{7,11},{8,12},{9,13},{1... | collective-permute-start | bytes 1572872 | tf_op jit(solution)/shard_map/ppermute | solution.py:71
  329.7 5.4 %collective-permute-start.29 = (bf16[8,128,256]{2,1,0:T(8,128)(2,1)}, bf16[8,128,256]{2,1,0:T(8,128)(2,1)}, u32[]{:S(2)}, u32[]{:S(2)}) collective-permute-start(bf16[8,128,256]{2,1,0:T(8,128)(2,1)} %get-tuple-element.32), channel_id=1, source_target_pairs={{0,8},{1,9},{2,10},{3,11},{4,12},{5,13},{6,14},{7,15},{8,0},{9,1},... | collective-permute-start | bytes 1572872 | tf_op jit(solution)/shard_map/ppermute | solution.py:71
  335.0 7.3 %collective-permute-done.15 = bf16[4,128,256]{2,1,0:T(8,128)(2,1)S(1)} collective-permute-done((bf16[4,128,256]{2,1,0:T(8,128)(2,1)S(1)}, bf16[4,128,256]{2,1,0:T(8,128)(2,1)S(1)}, u32[]{:S(2)}, u32[]{:S(2)}) %collective-permute-start.15) | collective-permute-done | bytes 262176 | tf_op jit(solution)/shard_map/ppermute | solution.py:88
  344.5 13.3 %collective-permute-done.16 = bf16[4,128,256]{2,1,0:T(8,128)(2,1)S(1)} collective-permute-done((bf16[4,128,256]{2,1,0:T(8,128)(2,1)S(1)}, bf16[4,128,256]{2,1,0:T(8,128)(2,1)S(1)}, u32[]{:S(2)}, u32[]{:S(2)}) %collective-permute-start.16) | collective-permute-done | bytes 262176 | tf_op jit(solution)/shard_map/ppermute | solution.py:88
  376.8 34.8 %collective-permute-start.31 = (bf16[256,768]{1,0:T(8,128)(2,1)S(1)}, bf16[256,768]{1,0:T(8,128)(2,1)S(1)}, u32[]{:S(2)}, u32[]{:S(2)}) collective-permute-start(bf16[256,768]{1,0:T(8,128)(2,1)S(1)} %fusion.35), channel_id=1, source_target_pairs={{0,496},{16,480},{32,464},{48,448},{64,432},{80,416},{96,400},{112... | collective-permute-start | bytes 1179656 | tf_op jit(solution)/shard_map/ppermute | solution.py:19
  411.7 17.4 %collective-permute-done.31 = bf16[256,768]{1,0:T(8,128)(2,1)S(1)} collective-permute-done((bf16[256,768]{1,0:T(8,128)(2,1)S(1)}, bf16[256,768]{1,0:T(8,128)(2,1)S(1)}, u32[]{:S(2)}, u32[]{:S(2)}) %collective-permute-start.31) | collective-permute-done | bytes 393248 | tf_op jit(solution)/shard_map/ppermute | solution.py:19
  (149 shorter events, 127.3 us)
Async XLA Ops:
  7.2 137.3 %all-gather.6.cloned.1.call-start = ((), (), s32[]{:S(2)}) async-start(), calls=%async_computation.1 | async-start | bytes 4456448 | tf_op jit(solution)/shard_map/all_gather | solution.py:135
  7.9 354.9 %all-gather.4.cloned.1.call-start = ((), (), s32[]{:S(2)}) async-start(), calls=%async_computation | async-start | bytes 2228224 | tf_op jit(solution)/shard_map/all_gather | solution.py:137
  9.1 25.6 %collective-permute-start = (bf16[128,256]{0,1:T(8,128)(2,1)S(1)}, bf16[128,256]{0,1:T(8,128)(2,1)S(1)}, u32[]{:S(2)}, u32[]{:S(2)}) collective-permute-start(bf16[128,256]{0,1:T(8,128)(2,1)S(1)} %get-tuple-element.40), channel_id=1, source_target_pairs={{0,1},{1,2},{2,3},{3,0},{4,5},{5,6},{6,7},{7,4},{8,9},{9,10},{10,1... | collective-permute-start | bytes 196616 | tf_op jit(solution)/shard_map/ppermute | solution.py:38
  168.7 25.6 %collective-permute-start.6 = (bf16[128,512]{1,0:T(8,128)(2,1)}, bf16[128,512]{1,0:T(8,128)(2,1)S(1)}, u32[]{:S(2)}, u32[]{:S(2)}) collective-permute-start(bf16[128,512]{1,0:T(8,128)(2,1)} %copy.48), channel_id=1, source_target_pairs={{0,1},{1,2},{2,3},{3,0},{4,5},{5,6},{6,7},{7,4},{8,9},{9,10},{10,1... | collective-permute-start | bytes 393224 | tf_op jit(solution)/shard_map/ppermute | solution.py:38
  172.2 33.7 %collective-permute-start.7 = (bf16[128,512]{1,0:T(8,128)(2,1)}, bf16[128,512]{1,0:T(8,128)(2,1)}, u32[]{:S(2)}, u32[]{:S(2)}) collective-permute-start(bf16[128,512]{1,0:T(8,128)(2,1)} %copy.48), channel_id=1, source_target_pairs={{0,2},{1,3},{2,0},{3,1},{4,6},{5,7},{6,4},{7,5},{8,10},{9,11},{10,... | collective-permute-start | bytes 393224 | tf_op jit(solution)/shard_map/ppermute | solution.py:38
  178.6 27.3 %collective-permute-start.8 = (bf16[128,512]{1,0:T(8,128)(2,1)}, bf16[128,512]{1,0:T(8,128)(2,1)}, u32[]{:S(2)}, u32[]{:S(2)}) collective-permute-start(bf16[128,512]{1,0:T(8,128)(2,1)} %copy.48), channel_id=1, source_target_pairs={{0,3},{1,0},{2,1},{3,2},{4,7},{5,4},{6,5},{7,6},{8,11},{9,8},{10,9... | collective-permute-start | bytes 393224 | tf_op jit(solution)/shard_map/ppermute | solution.py:38
  186.3 27.2 %collective-permute-start.18 = (bf16[4,128,256]{2,1,0:T(8,128)(2,1)}, bf16[4,128,256]{2,1,0:T(8,128)(2,1)}, u32[]{:S(2)}, u32[]{:S(2)}) collective-permute-start(bf16[4,128,256]{2,1,0:T(8,128)(2,1)} %bitcast.49), channel_id=1, source_target_pairs={{0,12},{1,13},{2,14},{3,15},{4,0},{5,1},{6,2},{7,3},{8,4},{9,5},{1... | collective-permute-start | bytes 786440 | tf_op jit(solution)/shard_map/ppermute | solution.py:48
  189.3 27.4 %collective-permute-start.19 = (bf16[4,128,256]{2,1,0:T(8,128)(2,1)}, bf16[4,128,256]{2,1,0:T(8,128)(2,1)}, u32[]{:S(2)}, u32[]{:S(2)}) collective-permute-start(bf16[4,128,256]{2,1,0:T(8,128)(2,1)} %bitcast.50), channel_id=1, source_target_pairs={{0,8},{1,9},{2,10},{3,11},{4,12},{5,13},{6,14},{7,15},{8,0},{9,1},... | collective-permute-start | bytes 786440 | tf_op jit(solution)/shard_map/ppermute | solution.py:48
  207.9 57.3 %collective-permute-start.9 = (bf16[4,128,512]{2,1,0:T(8,128)(2,1)}, bf16[4,128,512]{2,1,0:T(8,128)(2,1)}, u32[]{:S(2)}, u32[]{:S(2)}) collective-permute-start(bf16[4,128,512]{2,1,0:T(8,128)(2,1)} %get-tuple-element.30), channel_id=1, source_target_pairs={{0,4},{1,5},{2,6},{3,7},{4,8},{5,9},{6,10},{7,11},{8,12},{9,13},{1... | collective-permute-start | bytes 1572872 | tf_op jit(solution)/shard_map/ppermute | solution.py:40
  209.8 57.3 %collective-permute-start.10 = (bf16[4,128,512]{2,1,0:T(8,128)(2,1)}, bf16[4,128,512]{2,1,0:T(8,128)(2,1)}, u32[]{:S(2)}, u32[]{:S(2)}) collective-permute-start(bf16[4,128,512]{2,1,0:T(8,128)(2,1)} %get-tuple-element.30), channel_id=1, source_target_pairs={{0,8},{1,9},{2,10},{3,11},{4,12},{5,13},{6,14},{7,15},{8,0},{9,1},... | collective-permute-start | bytes 1572872 | tf_op jit(solution)/shard_map/ppermute | solution.py:40
  213.5 53.6 %collective-permute-start.11 = (bf16[4,128,512]{2,1,0:T(8,128)(2,1)}, bf16[4,128,512]{2,1,0:T(8,128)(2,1)}, u32[]{:S(2)}, u32[]{:S(2)}) collective-permute-start(bf16[4,128,512]{2,1,0:T(8,128)(2,1)} %get-tuple-element.30), channel_id=1, source_target_pairs={{0,12},{1,13},{2,14},{3,15},{4,0},{5,1},{6,2},{7,3},{8,4},{9,5},{1... | collective-permute-start | bytes 1572872 | tf_op jit(solution)/shard_map/ppermute | solution.py:40
  245.2 49.5 %collective-permute-start.25 = (bf16[5,128,256]{2,1,0:T(8,128)(2,1)S(1)}, bf16[5,128,256]{2,1,0:T(8,128)(2,1)S(1)}, u32[]{:S(2)}, u32[]{:S(2)}) collective-permute-start(bf16[5,128,256]{2,1,0:T(8,128)(2,1)S(1)} %get-tuple-element.42), channel_id=1, source_target_pairs={{0,1},{1,2},{2,3},{3,0},{4,5},{5,6},{6,7},{7,4},{8,9},{9,10},{10,1... | collective-permute-start | bytes 983048 | tf_op jit(solution)/shard_map/ppermute | solution.py:64
  257.2 43.4 %collective-permute-start.26 = (bf16[5,128,256]{2,1,0:T(8,128)(2,1)S(1)}, bf16[5,128,256]{2,1,0:T(8,128)(2,1)S(1)}, u32[]{:S(2)}, u32[]{:S(2)}) collective-permute-start(bf16[5,128,256]{2,1,0:T(8,128)(2,1)S(1)} %get-tuple-element.43), channel_id=1, source_target_pairs={{0,2},{1,3},{2,0},{3,1},{4,6},{5,7},{6,4},{7,5},{8,10},{9,11},{10,... | collective-permute-start | bytes 983048 | tf_op jit(solution)/shard_map/ppermute | solution.py:64
  265.2 35.5 %collective-permute-start.27 = (bf16[5,128,256]{2,1,0:T(8,128)(2,1)S(1)}, bf16[5,128,256]{2,1,0:T(8,128)(2,1)S(1)}, u32[]{:S(2)}, u32[]{:S(2)}) collective-permute-start(bf16[5,128,256]{2,1,0:T(8,128)(2,1)S(1)} %get-tuple-element.44), channel_id=1, source_target_pairs={{0,3},{1,0},{2,1},{3,2},{4,7},{5,4},{6,5},{7,6},{8,11},{9,8},{10,9... | collective-permute-start | bytes 983048 | tf_op jit(solution)/shard_map/ppermute | solution.py:64
  269.7 31.3 %collective-permute-start.12 = (bf16[4,128,256]{2,1,0:T(8,128)(2,1)S(1)}, bf16[4,128,256]{2,1,0:T(8,128)(2,1)S(1)}, u32[]{:S(2)}, u32[]{:S(2)}) collective-permute-start(bf16[4,128,256]{2,1,0:T(8,128)(2,1)S(1)} %bitcast.223), channel_id=1, source_target_pairs={{0,12},{1,13},{2,14},{3,15},{4,0},{5,1},{6,2},{7,3},{8,4},{9,5},{1... | collective-permute-start | bytes 786440 | tf_op jit(solution)/shard_map/ppermute | solution.py:84
  271.6 29.4 %collective-permute-start.13 = (bf16[4,128,256]{2,1,0:T(8,128)(2,1)S(1)}, bf16[4,128,256]{2,1,0:T(8,128)(2,1)S(1)}, u32[]{:S(2)}, u32[]{:S(2)}) collective-permute-start(bf16[4,128,256]{2,1,0:T(8,128)(2,1)S(1)} %bitcast.221), channel_id=1, source_target_pairs={{0,8},{1,9},{2,10},{3,11},{4,12},{5,13},{6,14},{7,15},{8,0},{9,1},... | collective-permute-start | bytes 786440 | tf_op jit(solution)/shard_map/ppermute | solution.py:84
  306.0 36.3 %collective-permute-start.15 = (bf16[4,128,256]{2,1,0:T(8,128)(2,1)S(1)}, bf16[4,128,256]{2,1,0:T(8,128)(2,1)S(1)}, u32[]{:S(2)}, u32[]{:S(2)}) collective-permute-start(bf16[4,128,256]{2,1,0:T(8,128)(2,1)S(1)} %get-tuple-element.16), channel_id=1, source_target_pairs={{0,3},{1,0},{2,1},{3,2},{4,7},{5,4},{6,5},{7,6},{8,11},{9,8},{10,9... | collective-permute-start | bytes 786440 | tf_op jit(solution)/shard_map/ppermute | solution.py:88
  311.0 46.8 %collective-permute-start.16 = (bf16[4,128,256]{2,1,0:T(8,128)(2,1)S(1)}, bf16[4,128,256]{2,1,0:T(8,128)(2,1)S(1)}, u32[]{:S(2)}, u32[]{:S(2)}) collective-permute-start(bf16[4,128,256]{2,1,0:T(8,128)(2,1)S(1)} %get-tuple-element.18), channel_id=1, source_target_pairs={{0,2},{1,3},{2,0},{3,1},{4,6},{5,7},{6,4},{7,5},{8,10},{9,11},{10,... | collective-permute-start | bytes 786440 | tf_op jit(solution)/shard_map/ppermute | solution.py:88
  316.1 41.7 %collective-permute-start.17 = (bf16[4,128,256]{2,1,0:T(8,128)(2,1)S(1)}, bf16[4,128,256]{2,1,0:T(8,128)(2,1)S(1)}, u32[]{:S(2)}, u32[]{:S(2)}) collective-permute-start(bf16[4,128,256]{2,1,0:T(8,128)(2,1)S(1)} %get-tuple-element.15), channel_id=1, source_target_pairs={{0,1},{1,2},{2,3},{3,0},{4,5},{5,6},{6,7},{7,4},{8,9},{9,10},{10,1... | collective-permute-start | bytes 786440 | tf_op jit(solution)/shard_map/ppermute | solution.py:88
  323.5 47.4 %collective-permute-start.28 = (bf16[8,128,256]{2,1,0:T(8,128)(2,1)}, bf16[8,128,256]{2,1,0:T(8,128)(2,1)}, u32[]{:S(2)}, u32[]{:S(2)}) collective-permute-start(bf16[8,128,256]{2,1,0:T(8,128)(2,1)} %get-tuple-element.31), channel_id=1, source_target_pairs={{0,4},{1,5},{2,6},{3,7},{4,8},{5,9},{6,10},{7,11},{8,12},{9,13},{1... | collective-permute-start | bytes 1572872 | tf_op jit(solution)/shard_map/ppermute | solution.py:71
  329.7 42.4 %collective-permute-start.29 = (bf16[8,128,256]{2,1,0:T(8,128)(2,1)}, bf16[8,128,256]{2,1,0:T(8,128)(2,1)}, u32[]{:S(2)}, u32[]{:S(2)}) collective-permute-start(bf16[8,128,256]{2,1,0:T(8,128)(2,1)} %get-tuple-element.32), channel_id=1, source_target_pairs={{0,8},{1,9},{2,10},{3,11},{4,12},{5,13},{6,14},{7,15},{8,0},{9,1},... | collective-permute-start | bytes 1572872 | tf_op jit(solution)/shard_map/ppermute | solution.py:71
  342.3 30.8 %collective-permute-start.30 = (bf16[8,128,256]{2,1,0:T(8,128)(2,1)}, bf16[8,128,256]{2,1,0:T(8,128)(2,1)}, u32[]{:S(2)}, u32[]{:S(2)}) collective-permute-start(bf16[8,128,256]{2,1,0:T(8,128)(2,1)} %get-tuple-element.33), channel_id=1, source_target_pairs={{0,12},{1,13},{2,14},{3,15},{4,0},{5,1},{6,2},{7,3},{8,4},{9,5},{1... | collective-permute-start | bytes 1572872 | tf_op jit(solution)/shard_map/ppermute | solution.py:71
  366.8 63.2 %collective-permute-start.24 = (bf16[128,4096]{1,0:T(8,128)(2,1)S(1)}, bf16[128,4096]{1,0:T(8,128)(2,1)S(1)}, u32[]{:S(2)}, u32[]{:S(2)}) collective-permute-start(bf16[128,4096]{1,0:T(8,128)(2,1)S(1)} %add_convert_fusion), channel_id=1, source_target_pairs={{0,16},{16,32},{32,48},{48,64},{64,80},{80,96},{96,112},{112,128},... | collective-permute-start | bytes 3145736 | tf_op jit(solution)/shard_map/ppermute | solution.py:14
  376.8 52.3 %collective-permute-start.31 = (bf16[256,768]{1,0:T(8,128)(2,1)S(1)}, bf16[256,768]{1,0:T(8,128)(2,1)S(1)}, u32[]{:S(2)}, u32[]{:S(2)}) collective-permute-start(bf16[256,768]{1,0:T(8,128)(2,1)S(1)} %fusion.35), channel_id=1, source_target_pairs={{0,496},{16,480},{32,464},{48,448},{64,432},{80,416},{96,400},{112... | collective-permute-start | bytes 1179656 | tf_op jit(solution)/shard_map/ppermute | solution.py:19
  (28 other events, 620.8 us)
Sparse Core Ops, SparseCore 0:
  11.0 133.4 all-gather.5
  147.5 135.8 all-gather.3
where the time goes:
time: 439 us; the launch traced here: 438 us
  starting transfers between devices  188 us (43%)
  waiting for transfers between devices  161 us (37%)
  matrix products  32.7 us (7%)
  local copies, waits for them, and re-layouts  22.6 us (5%)
  other arithmetic  18.5 us (4%)
  between operations  15.1 us (3%)
    all_gather x1, waiting for transfers between devices, per_device(): lax.all_gather(up_output_weight[0], 'seq', axis=1, tiled=True)  80.2 us
    ppermute x6, starting transfers between devices, gather_blocks(): lax.ppermute(x, 'seq', seq_pairs(k, 0))  40.2 us
    ppermute x1, starting transfers between devices, mirrored(): lax.ppermute(value, axis, [(source, count - 1 - source) for source in ran...  34.8 us
    ppermute x3, starting transfers between devices, gather_and_scatter(): lax.ppermute(jnp.concatenate([x, piece]), 'seq', seq_pairs(k, 0))  21.9 us
    ppermute x3, waiting for transfers between devices, gather_columns(): second.append(lax.ppermute(first[k], 'seq', seq_pairs(INNER - k, 0)))  20.5 us
    ppermute x6, starting transfers between devices, gather_blocks(): lax.ppermute(first, 'seq', seq_pairs(k, 1))  18.4 us
    ppermute x3, waiting for transfers between devices, gather_and_scatter(): lax.ppermute(jnp.concatenate([x, piece]), 'seq', seq_pairs(k, 0))  17.4 us
    ppermute x1, waiting for transfers between devices, mirrored(): lax.ppermute(value, axis, [(source, count - 1 - source) for source in ran...  17.4 us
  transfers between devices with their start and end apart: 34, of which 10 were waited for; matrix products, arithmetic and copies ran while one was open for 16% of the time, Pallas kernels for 0%

commit v1 on v0

--- a/solution.py
+++ b/solution.py
@@ -132,7 +132,9 @@
     cotangent = up_cotangent[0]
     unit_up, inverse_up, normed_up = normalize(up_activation[0], upward_gain[0])
     hidden = normed_up.astype(jnp.bfloat16)
-    output_weight = lax.all_gather(up_output_weight[0], "seq", axis=1, tiled=True)
+    output_weight = jnp.concatenate(
+        lax.all_to_all(jnp.stack([up_output_weight[0]] * lax.axis_size("seq")), "seq", 0, 0), axis=1
+    )
     key_value = gather_blocks(saved[:, width:]).reshape(size * count, 2 * HEAD)
     kv_weight_all = lax.all_gather(up_input_weight[0][:, width:], "seq", axis=0, tiled=True)
     keys = key_value[:, :HEAD]

time: 439 us -> 577 us (1.31)
  the two profiles are of different devices: /device:TPU:43 before, /device:TPU:68 now
where the time goes in v1:
time: 577 us; the launch traced here: 575 us
  waiting for transfers between devices  312 us (54%)
  starting transfers between devices  159 us (28%)
  matrix products  36.2 us (6%)
  local copies, waits for them, and re-layouts  28.1 us (5%)
  other arithmetic  23.8 us (4%)
  between operations  15 us (3%)
    ppermute x6, waiting for transfers between devices, gather_blocks(): lax.ppermute(x, 'seq', seq_pairs(k, 0))  222 us
    ppermute x6, starting transfers between devices, gather_blocks(): lax.ppermute(x, 'seq', seq_pairs(k, 0))  38.4 us
    ppermute x6, waiting for transfers between devices, gather_blocks(): lax.ppermute(first, 'seq', seq_pairs(k, 1))  27.9 us
    ppermute x1, waiting for transfers between devices, mirrored(): lax.ppermute(value, axis, [(source, count - 1 - source) for source in ran...  24.9 us
    ppermute x6, starting transfers between devices, gather_blocks(): lax.ppermute(first, 'seq', seq_pairs(k, 1))  18.2 us
    ppermute x3, starting transfers between devices, gather_and_scatter(): lax.ppermute(jnp.concatenate([x, piece]), 'seq', seq_pairs(k, 0))  17.8 us
    ppermute x3, starting transfers between devices, gather_columns(): second.append(lax.ppermute(first[k], 'seq', seq_pairs(INNER - k, 0)))  16.9 us
    all_to_all x1, starting transfers between devices, per_device(): lax.all_to_all(jnp.stack([up_output_weight[0]] * lax.axis_size('seq')), '...  16.4 us
  transfers between devices with their start and end apart: 34, of which 17 were waited for; matrix products, arithmetic and copies ran while one was open for 14% of the time, Pallas kernels for 0%

profile of v1, /device:TPU:68, one launch (start us, length us, event | category | flops | bytes accessed | tf_op | source)
XLA Modules:
  0.0 574.9 jit_solution(3548034808544211371)
XLA Ops:
  10.7 16.4 %all-to-all-start = ((bf16[16,512,256]{1,2,0:T(8,128)(2,1)}), bf16[16,512,256]{1,2,0:T(8,128)(2,1)}, u32[]{:S(2)}, u32[]{:S(2)}) async-start(bf16[16,512,256]{1,2,0:T(8,128)(2,1)} %stack.128), calls=%async_computation | async-start | bytes 8388608 | tf_op jit(solution)/shard_map/all_to_all | solution.py:136
  27.3 7.4 %collective-permute-start = (bf16[128,256]{0,1:T(8,128)(2,1)S(1)}, bf16[128,256]{0,1:T(8,128)(2,1)S(1)}, u32[]{:S(2)}, u32[]{:S(2)}) collective-permute-start(bf16[128,256]{0,1:T(8,128)(2,1)S(1)} %get-tuple-element.40), channel_id=1, source_target_pairs={{0,1},{1,2},{2,3},{3,0},{4,5},{5,6},{6,7},{7,4},{8,9},{9,10},{10,1... | collective-permute-start | bytes 196616 | tf_op jit(solution)/shard_map/ppermute | solution.py:38
  34.8 7.3 %collective-permute-start.1 = (bf16[128,256]{0,1:T(8,128)(2,1)S(1)}, bf16[128,256]{0,1:T(8,128)(2,1)S(1)}, u32[]{:S(2)}, u32[]{:S(2)}) collective-permute-start(bf16[128,256]{0,1:T(8,128)(2,1)S(1)} %get-tuple-element.40), channel_id=1, source_target_pairs={{0,2},{1,3},{2,0},{3,1},{4,6},{5,7},{6,4},{7,5},{8,10},{9,11},{10,... | collective-permute-start | bytes 196616 | tf_op jit(solution)/shard_map/ppermute | solution.py:38
  42.0 7.3 %collective-permute-start.2 = (bf16[128,256]{0,1:T(8,128)(2,1)S(1)}, bf16[128,256]{0,1:T(8,128)(2,1)S(1)}, u32[]{:S(2)}, u32[]{:S(2)}) collective-permute-start(bf16[128,256]{0,1:T(8,128)(2,1)S(1)} %get-tuple-element.40), channel_id=1, source_target_pairs={{0,3},{1,0},{2,1},{3,2},{4,7},{5,4},{6,5},{7,6},{8,11},{9,8},{10,9... | collective-permute-start | bytes 196616 | tf_op jit(solution)/shard_map/ppermute | solution.py:38
  52.3 175.7 %collective-permute-done = bf16[128,256]{0,1:T(8,128)(2,1)S(1)} collective-permute-done((bf16[128,256]{0,1:T(8,128)(2,1)S(1)}, bf16[128,256]{0,1:T(8,128)(2,1)S(1)}, u32[]{:S(2)}, u32[]{:S(2)}) %collective-permute-start) | collective-permute-done | bytes 65568 | tf_op jit(solution)/shard_map/ppermute | solution.py:38
  228.0 7.9 %collective-permute-done.1 = bf16[128,256]{0,1:T(8,128)(2,1)S(1)} collective-permute-done((bf16[128,256]{0,1:T(8,128)(2,1)S(1)}, bf16[128,256]{0,1:T(8,128)(2,1)S(1)}, u32[]{:S(2)}, u32[]{:S(2)}) %collective-permute-start.1) | collective-permute-done | bytes 65568 | tf_op jit(solution)/shard_map/ppermute | solution.py:38
  236.6 5.2 collective-permute-start.3
  265.3 5.4 fusion.83
  279.8 8.3 %convolution_bitcast_fusion.1 = f32[2048,128]{0,1:T(8,128)} fusion(bf16[128,4,128]{0,2,1:T(8,128)(2,1)S(1)} %bitcast.227, f32[128,4,2048]{0,2,1:T(8,128)} %fusion.59, f32[128,4,2048]{0,2,1:T(8,128)} %get-tuple-element.46, f32[128,4]{0,1:T(4,128)S(1)} %copy-done.21), kind=kOutput, calls=%fused_computation.25 | convolution fusion | flops 275778048 | bytes 9570304 | tf_op jit(solution)/shard_map/tgj,tgh->jh/dot_general | solution.py:171
  315.1 6.7 %collective-permute-start.21 = (bf16[128,256]{1,0:T(8,128)(2,1)S(1)}, bf16[128,256]{1,0:T(8,128)(2,1)S(1)}, u32[]{:S(2)}, u32[]{:S(2)}) collective-permute-start(bf16[128,256]{1,0:T(8,128)(2,1)S(1)} %get-tuple-element.34), channel_id=1, source_target_pairs={{0,3},{1,0},{2,1},{3,2},{4,7},{5,4},{6,5},{7,6},{8,11},{9,8},{10,9... | collective-permute-start | bytes 196616 | tf_op jit(solution)/shard_map/ppermute | solution.py:51
  324.5 6.7 %collective-permute-start.23 = (bf16[128,256]{1,0:T(8,128)(2,1)S(1)}, bf16[128,256]{1,0:T(8,128)(2,1)S(1)}, u32[]{:S(2)}, u32[]{:S(2)}) collective-permute-start(bf16[128,256]{1,0:T(8,128)(2,1)S(1)} %get-tuple-element.35), channel_id=1, source_target_pairs={{0,1},{1,2},{2,3},{3,0},{4,5},{5,6},{6,7},{7,4},{8,9},{9,10},{10,1... | collective-permute-start | bytes 196616 | tf_op jit(solution)/shard_map/ppermute | solution.py:51
  331.3 13.3 %collective-permute-done.22 = bf16[128,256]{1,0:T(8,128)(2,1)S(1)} collective-permute-done((bf16[128,256]{1,0:T(8,128)(2,1)S(1)}, bf16[128,256]{1,0:T(8,128)(2,1)S(1)}, u32[]{:S(2)}, u32[]{:S(2)}) %collective-permute-start.22) | collective-permute-done | bytes 65568 | tf_op jit(solution)/shard_map/ppermute | solution.py:51
  345.9 6.7 %collective-permute-start.25 = (bf16[5,128,256]{2,1,0:T(8,128)(2,1)}, bf16[5,128,256]{2,1,0:T(8,128)(2,1)S(1)}, u32[]{:S(2)}, u32[]{:S(2)}) collective-permute-start(bf16[5,128,256]{2,1,0:T(8,128)(2,1)} %get-tuple-element.42), channel_id=1, source_target_pairs={{0,1},{1,2},{2,3},{3,0},{4,5},{5,6},{6,7},{7,4},{8,9},{9,10},{10,1... | collective-permute-start | bytes 983048 | tf_op jit(solution)/shard_map/ppermute | solution.py:64
  352.6 7.2 %fusion.36 = bf16[128,4,128]{0,2,1:T(8,128)(2,1)S(1)} fusion(f32[128,4,2048]{0,2,1:T(8,128)} %fusion.59, bf16[2048,256]{1,0:T(8,128)(2,1)S(1)} %bitcast.196, f32[128,4,2048]{0,2,1:T(8,128)} %get-tuple-element.46, f32[128,4]{0,1:T(4,128)} %get-tuple-element.45), kind=kOutput, calls=%fused_computation.57 | convolution fusion | flops 275843584 | bytes 17436672 | tf_op jit(solution)/shard_map/tgj,jh->tgh/dot_general | solution.py:167
  362.9 7.5 %collective-permute-start.7 = (bf16[128,512]{1,0:T(8,128)(2,1)S(1)}, bf16[128,512]{1,0:T(8,128)(2,1)S(1)}, u32[]{:S(2)}, u32[]{:S(2)}) collective-permute-start(bf16[128,512]{1,0:T(8,128)(2,1)S(1)} %copy.49), channel_id=1, source_target_pairs={{0,2},{1,3},{2,0},{3,1},{4,6},{5,7},{6,4},{7,5},{8,10},{9,11},{10,... | collective-permute-start | bytes 393224 | tf_op jit(solution)/shard_map/ppermute | solution.py:38
  370.5 5.9 %collective-permute-start.8 = (bf16[128,512]{1,0:T(8,128)(2,1)S(1)}, bf16[128,512]{1,0:T(8,128)(2,1)S(1)}, u32[]{:S(2)}, u32[]{:S(2)}) collective-permute-start(bf16[128,512]{1,0:T(8,128)(2,1)S(1)} %copy.49), channel_id=1, source_target_pairs={{0,3},{1,0},{2,1},{3,2},{4,7},{5,4},{6,5},{7,6},{8,11},{9,8},{10,9... | collective-permute-start | bytes 393224 | tf_op jit(solution)/shard_map/ppermute | solution.py:38
  376.4 7.9 %collective-permute-start.26 = (bf16[5,128,256]{2,1,0:T(8,128)(2,1)}, bf16[5,128,256]{2,1,0:T(8,128)(2,1)S(1)}, u32[]{:S(2)}, u32[]{:S(2)}) collective-permute-start(bf16[5,128,256]{2,1,0:T(8,128)(2,1)} %get-tuple-element.43), channel_id=1, source_target_pairs={{0,2},{1,3},{2,0},{3,1},{4,6},{5,7},{6,4},{7,5},{8,10},{9,11},{10,... | collective-permute-start | bytes 983048 | tf_op jit(solution)/shard_map/ppermute | solution.py:64
  387.7 38.2 %collective-permute-done.8 = bf16[128,512]{1,0:T(8,128)(2,1)S(1)} collective-permute-done((bf16[128,512]{1,0:T(8,128)(2,1)S(1)}, bf16[128,512]{1,0:T(8,128)(2,1)S(1)}, u32[]{:S(2)}, u32[]{:S(2)}) %collective-permute-start.8) | collective-permute-done | bytes 131104 | tf_op jit(solution)/shard_map/ppermute | solution.py:38
  436.5 18.8 %collective-permute-done.9 = bf16[4,128,512]{2,1,0:T(8,128)(2,1)} collective-permute-done((bf16[4,128,512]{2,1,0:T(8,128)(2,1)}, bf16[4,128,512]{2,1,0:T(8,128)(2,1)}, u32[]{:S(2)}, u32[]{:S(2)}) %collective-permute-start.9) | collective-permute-done | bytes 524320 | tf_op jit(solution)/shard_map/ppermute | solution.py:40
  471.8 4.5 collective-permute-start.28
  488.9 8.8 %collective-permute-start.16 = (bf16[4,128,256]{2,1,0:T(8,128)(2,1)S(1)}, bf16[4,128,256]{2,1,0:T(8,128)(2,1)S(1)}, u32[]{:S(2)}, u32[]{:S(2)}) collective-permute-start(bf16[4,128,256]{2,1,0:T(8,128)(2,1)S(1)} %get-tuple-element.18), channel_id=1, source_target_pairs={{0,2},{1,3},{2,0},{3,1},{4,6},{5,7},{6,4},{7,5},{8,10},{9,11},{10,... | collective-permute-start | bytes 786440 | tf_op jit(solution)/shard_map/ppermute | solution.py:88
  511.6 8.2 %collective-permute-done.16 = bf16[4,128,256]{2,1,0:T(8,128)(2,1)S(1)} collective-permute-done((bf16[4,128,256]{2,1,0:T(8,128)(2,1)S(1)}, bf16[4,128,256]{2,1,0:T(8,128)(2,1)S(1)}, u32[]{:S(2)}, u32[]{:S(2)}) %collective-permute-start.16) | collective-permute-done | bytes 262176 | tf_op jit(solution)/shard_map/ppermute | solution.py:88
  535.6 5.8 %collective-permute-start.31 = (bf16[256,768]{1,0:T(8,128)(2,1)S(1)}, bf16[256,768]{1,0:T(8,128)(2,1)S(1)}, u32[]{:S(2)}, u32[]{:S(2)}) collective-permute-start(bf16[256,768]{1,0:T(8,128)(2,1)S(1)} %fusion.33), channel_id=1, source_target_pairs={{0,496},{16,480},{32,464},{48,448},{64,432},{80,416},{96,400},{112... | collective-permute-start | bytes 1179656 | tf_op jit(solution)/shard_map/ppermute | solution.py:19
  541.4 24.9 %collective-permute-done.31 = bf16[256,768]{1,0:T(8,128)(2,1)S(1)} collective-permute-done((bf16[256,768]{1,0:T(8,128)(2,1)S(1)}, bf16[256,768]{1,0:T(8,128)(2,1)S(1)}, u32[]{:S(2)}, u32[]{:S(2)}) %collective-permute-start.31) | collective-permute-done | bytes 393248 | tf_op jit(solution)/shard_map/ppermute | solution.py:19
  (158 shorter events, 148.1 us)
Async XLA Ops:
  10.7 260.1 %all-to-all-start = ((bf16[16,512,256]{1,2,0:T(8,128)(2,1)}), bf16[16,512,256]{1,2,0:T(8,128)(2,1)}, u32[]{:S(2)}, u32[]{:S(2)}) async-start(bf16[16,512,256]{1,2,0:T(8,128)(2,1)} %stack.128), calls=%async_computation | async-start | bytes 8388608 | tf_op jit(solution)/shard_map/all_to_all | solution.py:136
  27.1 500.1 %all-gather.2.cloned.1.call-start = ((), (), s32[]{:S(2)}) async-start(), calls=%async_computation.1 | async-start | bytes 2228224 | tf_op jit(solution)/shard_map/all_gather | solution.py:139
  27.3 200.6 %collective-permute-start = (bf16[128,256]{0,1:T(8,128)(2,1)S(1)}, bf16[128,256]{0,1:T(8,128)(2,1)S(1)}, u32[]{:S(2)}, u32[]{:S(2)}) collective-permute-start(bf16[128,256]{0,1:T(8,128)(2,1)S(1)} %get-tuple-element.40), channel_id=1, source_target_pairs={{0,1},{1,2},{2,3},{3,0},{4,5},{5,6},{6,7},{7,4},{8,9},{9,10},{10,1... | collective-permute-start | bytes 196616 | tf_op jit(solution)/shard_map/ppermute | solution.py:38
  34.8 201.1 %collective-permute-start.1 = (bf16[128,256]{0,1:T(8,128)(2,1)S(1)}, bf16[128,256]{0,1:T(8,128)(2,1)S(1)}, u32[]{:S(2)}, u32[]{:S(2)}) collective-permute-start(bf16[128,256]{0,1:T(8,128)(2,1)S(1)} %get-tuple-element.40), channel_id=1, source_target_pairs={{0,2},{1,3},{2,0},{3,1},{4,6},{5,7},{6,4},{7,5},{8,10},{9,11},{10,... | collective-permute-start | bytes 196616 | tf_op jit(solution)/shard_map/ppermute | solution.py:38
  42.0 193.8 %collective-permute-start.2 = (bf16[128,256]{0,1:T(8,128)(2,1)S(1)}, bf16[128,256]{0,1:T(8,128)(2,1)S(1)}, u32[]{:S(2)}, u32[]{:S(2)}) collective-permute-start(bf16[128,256]{0,1:T(8,128)(2,1)S(1)} %get-tuple-element.40), channel_id=1, source_target_pairs={{0,3},{1,0},{2,1},{3,2},{4,7},{5,4},{6,5},{7,6},{8,11},{9,8},{10,9... | collective-permute-start | bytes 196616 | tf_op jit(solution)/shard_map/ppermute | solution.py:38
  321.8 22.8 %collective-permute-start.22 = (bf16[128,256]{1,0:T(8,128)(2,1)S(1)}, bf16[128,256]{1,0:T(8,128)(2,1)S(1)}, u32[]{:S(2)}, u32[]{:S(2)}) collective-permute-start(bf16[128,256]{1,0:T(8,128)(2,1)S(1)} %get-tuple-element.36), channel_id=1, source_target_pairs={{0,2},{1,3},{2,0},{3,1},{4,6},{5,7},{6,4},{7,5},{8,10},{9,11},{10,... | collective-permute-start | bytes 196616 | tf_op jit(solution)/shard_map/ppermute | solution.py:51
  324.5 20.4 %collective-permute-start.23 = (bf16[128,256]{1,0:T(8,128)(2,1)S(1)}, bf16[128,256]{1,0:T(8,128)(2,1)S(1)}, u32[]{:S(2)}, u32[]{:S(2)}) collective-permute-start(bf16[128,256]{1,0:T(8,128)(2,1)S(1)} %get-tuple-element.35), channel_id=1, source_target_pairs={{0,1},{1,2},{2,3},{3,0},{4,5},{5,6},{6,7},{7,4},{8,9},{9,10},{10,1... | collective-permute-start | bytes 196616 | tf_op jit(solution)/shard_map/ppermute | solution.py:51
  345.9 87.6 %collective-permute-start.25 = (bf16[5,128,256]{2,1,0:T(8,128)(2,1)}, bf16[5,128,256]{2,1,0:T(8,128)(2,1)S(1)}, u32[]{:S(2)}, u32[]{:S(2)}) collective-permute-start(bf16[5,128,256]{2,1,0:T(8,128)(2,1)} %get-tuple-element.42), channel_id=1, source_target_pairs={{0,1},{1,2},{2,3},{3,0},{4,5},{5,6},{6,7},{7,4},{8,9},{9,10},{10,1... | collective-permute-start | bytes 983048 | tf_op jit(solution)/shard_map/ppermute | solution.py:64
  359.9 24.3 %collective-permute-start.6 = (bf16[128,512]{1,0:T(8,128)(2,1)S(1)}, bf16[128,512]{1,0:T(8,128)(2,1)S(1)}, u32[]{:S(2)}, u32[]{:S(2)}) collective-permute-start(bf16[128,512]{1,0:T(8,128)(2,1)S(1)} %copy.49), channel_id=1, source_target_pairs={{0,1},{1,2},{2,3},{3,0},{4,5},{5,6},{6,7},{7,4},{8,9},{9,10},{10,1... | collective-permute-start | bytes 393224 | tf_op jit(solution)/shard_map/ppermute | solution.py:38
  362.9 24.7 %collective-permute-start.7 = (bf16[128,512]{1,0:T(8,128)(2,1)S(1)}, bf16[128,512]{1,0:T(8,128)(2,1)S(1)}, u32[]{:S(2)}, u32[]{:S(2)}) collective-permute-start(bf16[128,512]{1,0:T(8,128)(2,1)S(1)} %copy.49), channel_id=1, source_target_pairs={{0,2},{1,3},{2,0},{3,1},{4,6},{5,7},{6,4},{7,5},{8,10},{9,11},{10,... | collective-permute-start | bytes 393224 | tf_op jit(solution)/shard_map/ppermute | solution.py:38
  370.5 55.4 %collective-permute-start.8 = (bf16[128,512]{1,0:T(8,128)(2,1)S(1)}, bf16[128,512]{1,0:T(8,128)(2,1)S(1)}, u32[]{:S(2)}, u32[]{:S(2)}) collective-permute-start(bf16[128,512]{1,0:T(8,128)(2,1)S(1)} %copy.49), channel_id=1, source_target_pairs={{0,3},{1,0},{2,1},{3,2},{4,7},{5,4},{6,5},{7,6},{8,11},{9,8},{10,9... | collective-permute-start | bytes 393224 | tf_op jit(solution)/shard_map/ppermute | solution.py:38
  376.4 59.7 %collective-permute-start.26 = (bf16[5,128,256]{2,1,0:T(8,128)(2,1)}, bf16[5,128,256]{2,1,0:T(8,128)(2,1)S(1)}, u32[]{:S(2)}, u32[]{:S(2)}) collective-permute-start(bf16[5,128,256]{2,1,0:T(8,128)(2,1)} %get-tuple-element.43), channel_id=1, source_target_pairs={{0,2},{1,3},{2,0},{3,1},{4,6},{5,7},{6,4},{7,5},{8,10},{9,11},{10,... | collective-permute-start | bytes 983048 | tf_op jit(solution)/shard_map/ppermute | solution.py:64
  384.3 51.9 %collective-permute-start.27 = (bf16[5,128,256]{2,1,0:T(8,128)(2,1)}, bf16[5,128,256]{2,1,0:T(8,128)(2,1)S(1)}, u32[]{:S(2)}, u32[]{:S(2)}) collective-permute-start(bf16[5,128,256]{2,1,0:T(8,128)(2,1)} %get-tuple-element.44), channel_id=1, source_target_pairs={{0,3},{1,0},{2,1},{3,2},{4,7},{5,4},{6,5},{7,6},{8,11},{9,8},{10,9... | collective-permute-start | bytes 983048 | tf_op jit(solution)/shard_map/ppermute | solution.py:64
  428.3 27.1 %collective-permute-start.9 = (bf16[4,128,512]{2,1,0:T(8,128)(2,1)}, bf16[4,128,512]{2,1,0:T(8,128)(2,1)}, u32[]{:S(2)}, u32[]{:S(2)}) collective-permute-start(bf16[4,128,512]{2,1,0:T(8,128)(2,1)} %get-tuple-element.30), channel_id=1, source_target_pairs={{0,4},{1,5},{2,6},{3,7},{4,8},{5,9},{6,10},{7,11},{8,12},{9,13},{1... | collective-permute-start | bytes 1572872 | tf_op jit(solution)/shard_map/ppermute | solution.py:40
  430.2 25.2 %collective-permute-start.10 = (bf16[4,128,512]{2,1,0:T(8,128)(2,1)}, bf16[4,128,512]{2,1,0:T(8,128)(2,1)}, u32[]{:S(2)}, u32[]{:S(2)}) collective-permute-start(bf16[4,128,512]{2,1,0:T(8,128)(2,1)} %get-tuple-element.30), channel_id=1, source_target_pairs={{0,8},{1,9},{2,10},{3,11},{4,12},{5,13},{6,14},{7,15},{8,0},{9,1},... | collective-permute-start | bytes 1572872 | tf_op jit(solution)/shard_map/ppermute | solution.py:40
  433.5 25.6 %collective-permute-start.11 = (bf16[4,128,512]{2,1,0:T(8,128)(2,1)}, bf16[4,128,512]{2,1,0:T(8,128)(2,1)}, u32[]{:S(2)}, u32[]{:S(2)}) collective-permute-start(bf16[4,128,512]{2,1,0:T(8,128)(2,1)} %get-tuple-element.30), channel_id=1, source_target_pairs={{0,12},{1,13},{2,14},{3,15},{4,0},{5,1},{6,2},{7,3},{8,4},{9,5},{1... | collective-permute-start | bytes 1572872 | tf_op jit(solution)/shard_map/ppermute | solution.py:40
  471.8 25.9 %collective-permute-start.28 = (bf16[8,128,256]{2,1,0:T(8,128)(2,1)S(1)}, bf16[8,128,256]{2,1,0:T(8,128)(2,1)}, u32[]{:S(2)}, u32[]{:S(2)}) collective-permute-start(bf16[8,128,256]{2,1,0:T(8,128)(2,1)S(1)} %get-tuple-element.31), channel_id=1, source_target_pairs={{0,4},{1,5},{2,6},{3,7},{4,8},{5,9},{6,10},{7,11},{8,12},{9,13},{1... | collective-permute-start | bytes 1572872 | tf_op jit(solution)/shard_map/ppermute | solution.py:71
  476.4 29.1 %collective-permute-start.29 = (bf16[8,128,256]{2,1,0:T(8,128)(2,1)S(1)}, bf16[8,128,256]{2,1,0:T(8,128)(2,1)S(1)}, u32[]{:S(2)}, u32[]{:S(2)}) collective-permute-start(bf16[8,128,256]{2,1,0:T(8,128)(2,1)S(1)} %get-tuple-element.32), channel_id=1, source_target_pairs={{0,8},{1,9},{2,10},{3,11},{4,12},{5,13},{6,14},{7,15},{8,0},{9,1},... | collective-permute-start | bytes 1572872 | tf_op jit(solution)/shard_map/ppermute | solution.py:71
  478.3 27.9 %collective-permute-start.30 = (bf16[8,128,256]{2,1,0:T(8,128)(2,1)S(1)}, bf16[8,128,256]{2,1,0:T(8,128)(2,1)S(1)}, u32[]{:S(2)}, u32[]{:S(2)}) collective-permute-start(bf16[8,128,256]{2,1,0:T(8,128)(2,1)S(1)} %get-tuple-element.33), channel_id=1, source_target_pairs={{0,12},{1,13},{2,14},{3,15},{4,0},{5,1},{6,2},{7,3},{8,4},{9,5},{1... | collective-permute-start | bytes 1572872 | tf_op jit(solution)/shard_map/ppermute | solution.py:71
  484.5 27.1 %collective-permute-start.15 = (bf16[4,128,256]{2,1,0:T(8,128)(2,1)S(1)}, bf16[4,128,256]{2,1,0:T(8,128)(2,1)S(1)}, u32[]{:S(2)}, u32[]{:S(2)}) collective-permute-start(bf16[4,128,256]{2,1,0:T(8,128)(2,1)S(1)} %get-tuple-element.16), channel_id=1, source_target_pairs={{0,3},{1,0},{2,1},{3,2},{4,7},{5,4},{6,5},{7,6},{8,11},{9,8},{10,9... | collective-permute-start | bytes 786440 | tf_op jit(solution)/shard_map/ppermute | solution.py:88
  488.9 30.9 %collective-permute-start.16 = (bf16[4,128,256]{2,1,0:T(8,128)(2,1)S(1)}, bf16[4,128,256]{2,1,0:T(8,128)(2,1)S(1)}, u32[]{:S(2)}, u32[]{:S(2)}) collective-permute-start(bf16[4,128,256]{2,1,0:T(8,128)(2,1)S(1)} %get-tuple-element.18), channel_id=1, source_target_pairs={{0,2},{1,3},{2,0},{3,1},{4,6},{5,7},{6,4},{7,5},{8,10},{9,11},{10,... | collective-permute-start | bytes 786440 | tf_op jit(solution)/shard_map/ppermute | solution.py:88
  497.7 24.5 %collective-permute-start.17 = (bf16[4,128,256]{2,1,0:T(8,128)(2,1)S(1)}, bf16[4,128,256]{2,1,0:T(8,128)(2,1)S(1)}, u32[]{:S(2)}, u32[]{:S(2)}) collective-permute-start(bf16[4,128,256]{2,1,0:T(8,128)(2,1)S(1)} %get-tuple-element.15), channel_id=1, source_target_pairs={{0,1},{1,2},{2,3},{3,0},{4,5},{5,6},{6,7},{7,4},{8,9},{9,10},{10,1... | collective-permute-start | bytes 786440 | tf_op jit(solution)/shard_map/ppermute | solution.py:88
  531.2 35.9 %collective-permute-start.24 = (bf16[128,4096]{1,0:T(8,128)(2,1)S(1)}, bf16[128,4096]{1,0:T(8,128)(2,1)S(1)}, u32[]{:S(2)}, u32[]{:S(2)}) collective-permute-start(bf16[128,4096]{1,0:T(8,128)(2,1)S(1)} %add_convert_fusion), channel_id=1, source_target_pairs={{0,16},{16,32},{32,48},{48,64},{64,80},{80,96},{96,112},{112,128},... | collective-permute-start | bytes 3145736 | tf_op jit(solution)/shard_map/ppermute | solution.py:14
  535.6 30.7 %collective-permute-start.31 = (bf16[256,768]{1,0:T(8,128)(2,1)S(1)}, bf16[256,768]{1,0:T(8,128)(2,1)S(1)}, u32[]{:S(2)}, u32[]{:S(2)}) collective-permute-start(bf16[256,768]{1,0:T(8,128)(2,1)S(1)} %fusion.33), channel_id=1, source_target_pairs={{0,496},{16,480},{32,464},{48,448},{64,432},{80,416},{96,400},{112... | collective-permute-start | bytes 1179656 | tf_op jit(solution)/shard_map/ppermute | solution.py:19
  (32 other events, 620.4 us)
Sparse Core Ops, SparseCore 0:
  51.0 228.3 all-gather.1
